TPU v7x, 512 devices: a whole 4x8x8 slice. The times are simulated.
512 devices in a mesh: req: 64 (over z, x, core), voc: 8 (over y).
Axes of the slice: x: 4, y: 8, z: 8, core: 2. Of those that a mesh axis runs over, the one named last changes fastest.
Arguments:
- hidden: bfloat16 [65536, 1600], P(('req', 'voc')), may hold values from -60 to 60
- norm_gain: float32 [1600], replicated, may hold values from 0.25 to 1.75
- unembed: bfloat16 [16384, 1600], P(('req', 'voc')), may hold values from -2 to 2
- targets: int32 [65536], P(('req', 'voc')), may hold values from 0 to 16383
- live: int32 [65536], P(('req', 'voc')), may hold values from 0 to 1, as said below
Outputs:
- logprob: float32 [65536], P(('req', 'voc'))
- entropy: float32 [65536], P(('req', 'voc'))
Inputs may be any that keep to these rules, and one draw needn't show every extreme that they name: Within each aligned block of 1024 slots (one owner's) the live slots form a prefix of 128 to 1024 slots, and in every draw at least one block is wholly live.
All inputs are finite; a program needn't handle non-finite values.
Results may differ from a plain program's by a relative error of at most 0.0067.
Values may be sent and summed in bfloat16 or wider, within the bound.
No kernel may reach another device: no remote copies, remote signals or barrier semaphores. Data moves between devices by JAX's collectives and lax.ppermute only.
A program may use at most 64 MiB of HBM per device.

v0:
```python
import jax
import jax.numpy as jnp
from jax import lax
from jax.sharding import PartitionSpec as P


def merged_2(value, axis, join):
    pieces = jax.tree.map(lambda part: lax.all_gather(part, axis), value)
    head = jax.tree.map(lambda part: part[0], pieces)
    tail = jax.tree.map(lambda part: part[1:], pieces)
    so_far, _ = lax.scan(lambda so_far, piece: (join(so_far, piece), None), head, tail)
    return so_far


def combine_stats(first, second):
    top = jnp.maximum(first[0], second[0])
    scale_one = jnp.exp(first[0] - top)
    scale_two = jnp.exp(second[0] - top)
    total = first[1] * scale_one + second[1] * scale_two
    spread = scale_one * (first[2] + (first[0] - top) * first[1]) + scale_two * (
        second[2] + (second[0] - top) * second[1]
    )
    return (top, total, spread, first[3] + second[3])


def on_device(hidden, norm_gain, unembed, targets, live):
    rows, wanted = (
        lax.all_gather(hidden, "voc", axis=0, tiled=True),
        lax.all_gather(targets, "voc", axis=0, tiled=True),
    )
    wide = rows.astype(jnp.float32)
    normed = (
        wide * lax.rsqrt(jnp.mean(wide * wide, axis=1, keepdims=True) + 1e-06) * norm_gain
    ).astype(jnp.bfloat16)
    groups = lax.axis_size("voc")
    column = lax.axis_index("voc")
    width = unembed.shape[0]
    count = normed.shape[0]
    zeros = jnp.zeros((count,), jnp.float32)
    start_carry = (jnp.full((count,), -1e30, jnp.float32), zeros, zeros, zeros)
    whole = lax.all_gather(unembed, "req", axis=0, tiled=True)
    stats = start_carry
    step = min(512, whole.shape[0])
    for first in range(0, whole.shape[0], step):
        piece = whole[first : first + step]
        logits = lax.dot_general(
            normed, piece, (((1,), (1,)), ((), ())), preferred_element_type=jnp.float32
        )
        local = first + jnp.arange(piece.shape[0], dtype=jnp.int32)
        vocab_ids = local // width * (groups * width) + column * width + local % width
        chosen = jnp.sum(jnp.where(vocab_ids[None, :] == wanted[:, None], logits, 0.0), axis=1)
        fold_top = jnp.max(logits, axis=1)
        shifted = logits - fold_top[:, None]
        weights = jnp.exp(shifted)
        newer = (fold_top, jnp.sum(weights, axis=1), jnp.sum(weights * shifted, axis=1), chosen)
        stats = combine_stats(stats, newer)
    mine = count // groups
    merged = merged_2(stats, "voc", combine_stats)
    top = lax.dynamic_slice_in_dim(merged[0], column * mine, mine)
    total = lax.dynamic_slice_in_dim(merged[1], column * mine, mine)
    spread = lax.dynamic_slice_in_dim(merged[2], column * mine, mine)
    picked = lax.dynamic_slice_in_dim(merged[3], column * mine, mine)
    mask = live.astype(jnp.float32)
    logprob = (picked - top - jnp.log(total)) * mask
    entropy = (jnp.log(total) - spread / total) * mask
    return (logprob, entropy)


def solution(mesh):
    return jax.shard_map(
        on_device,
        mesh=mesh,
        in_specs=(
            P(("req", "voc"), None),
            P(),
            P(("req", "voc"), None),
            P(("req", "voc")),
            P(("req", "voc")),
        ),
        out_specs=(P(("req", "voc")), P(("req", "voc"))),
        check_vma=False,
    )
```

profile of v0, /device:TPU:16, one launch (start us, length us, event | category | flops | bytes accessed | tf_op | source)
XLA Modules:
  0.0 284.1 jit_solution(10954525450019727820)
XLA Ops:
  7.2 0.0 copy-start.3
  7.2 0.0 all-gather.8.cloned.1.call-start
  7.2 0.7 all-gather.8.cloned.1.call-update
  7.9 0.0 all-gather.10.cloned.1.call-start
  8.0 0.7 all-gather.10.cloned.1.call-update
  8.7 16.5 %all-gather.4 = s32[8,1,128]{2,1,0:T(1,128)S(1)} all-gather(s32[1,1,128]{2,1,0:T(1,128)} %bitcast.74), channel_id=1, replica_groups=mesh['req'=64,'voc'=8] {'voc'}, dimensions={0}, use_global_device_ids=true | all-gather | bytes 4608 | tf_op jit(solution)/shard_map/all_gather | solution.py:29
  25.1 46.9 %all-gather.8.cloned.1.call-done = bf16[1024,1600]{0,1:T(8,128)(2,1)} async-done(((bf16[128,1600]{0,1:T(8,128)(2,1)}), bf16[1024,1600]{0,1:T(8,128)(2,1)}) %all-gather.8.cloned.1.call-update) | async-done | bytes 3276816 | tf_op jit(solution)/shard_map/all_gather | solution.py:28
  72.1 0.0 copy-start
  72.1 2.8 fusion
  74.9 87.4 %all-gather.10.cloned.1.call-done = bf16[2048,1600]{1,0:T(8,128)(2,1)} async-done(((bf16[32,1600]{1,0:T(8,128)(2,1)}), bf16[2048,1600]{1,0:T(8,128)(2,1)}) %all-gather.10.cloned.1.call-update) | async-done | bytes 6553616 | tf_op jit(solution)/shard_map/all_gather | solution.py:41
  162.3 0.0 copy-done.3
  162.3 0.0 copy-done
  162.3 0.0 copy-start.2
  162.3 3.8 %fusion.44 = (f32[1024]{0:T(1024)S(1)}, f32[1024,512]{0,1:T(8,128)S(1)}) fusion(bf16[1024,1600]{0,1:T(8,128)(2,1)S(1)} %copy-done, f32[1600]{0:T(1024)S(1)} %copy-done.3, f32[1024]{0:T(1024)S(1)} %add_rsqrt_fusion, bf16[2048,1600]{1,0:T(8,128)(2,1)} %all-gather.10.cloned.1.call-done), kind=kOutput, calls=%fused_computation.103 | convolution fusion | flops 1684798464 | bytes 7092480 | tf_op jit(solution)/shard_map/dot_general | solution.py:46
  166.2 0.0 copy-done.2
  166.2 2.2 fusion.45
  168.4 2.2 fusion.46
  170.7 2.2 fusion.47
  172.9 0.0 copy-start.1
  173.0 3.9 %fusion.3 = (f32[1024]{0:T(1024)S(1)}, f32[1024]{0:T(1024)S(1)}, f32[1024]{0:T(1024)S(1)}, f32[1024]{0:T(1024)S(1)}, f32[1024]{0:T(1024)S(1)}, /*index=5*/f32[10...) fusion(f32[1024,512]{0,1:T(8,128)S(1)} %get-tuple-element.108, ...), kind=kLoop, calls=%fused_computation.19 | loop fusion | flops 14667776 | bytes 8466432 | tf_op jit(solution)/shard_map/reduce_sum | solution.py:55
  176.9 25.4 %all-gather = f32[8192]{0:T(1024)S(1)} all-gather(f32[1024]{0:T(1024)S(1)} %add_add_fusion), channel_id=2, replica_groups=mesh['req'=64,'voc'=8] {'voc'}, dimensions={0}, use_global_device_ids=true | all-gather | bytes 36864 | tf_op jit(solution)/shard_map/all_gather | solution.py:8
  202.3 0.1 add_bitcast_fusion
  202.4 24.5 %all-gather.2 = f32[8,1,1024]{2,1,0:T(1,128)S(1)} all-gather(f32[1,1,1024]{2,1,0:T(1,128)S(1)} %get-tuple-element.94), channel_id=1, replica_groups=mesh['req'=64,'voc'=8] {'voc'}, dimensions={0}, use_global_device_ids=true | all-gather | bytes 36864 | tf_op jit(solution)/shard_map/all_gather | solution.py:8
  226.9 24.5 %all-gather.1 = f32[8,1,1024]{2,1,0:T(1,128)S(1)} all-gather(f32[1,1,1024]{2,1,0:T(1,128)S(1)} %get-tuple-element.95), channel_id=1, replica_groups=mesh['req'=64,'voc'=8] {'voc'}, dimensions={0}, use_global_device_ids=true | all-gather | bytes 36864 | tf_op jit(solution)/shard_map/all_gather | solution.py:8
  251.3 24.5 %all-gather.3 = f32[8,1,1024]{2,1,0:T(1,128)S(1)} all-gather(f32[1,1,1024]{2,1,0:T(1,128)S(1)} %get-tuple-element.88), channel_id=1, replica_groups=mesh['req'=64,'voc'=8] {'voc'}, dimensions={0}, use_global_device_ids=true | all-gather | bytes 36864 | tf_op jit(solution)/shard_map/all_gather | solution.py:8
  275.8 0.8 while.16
  276.7 0.0 copy-done.1
  276.7 0.6 subtract_multiply_fusion
  (59 shorter events, 0.5 us)
Async XLA Ops:
  7.2 155.2 %copy-start.3 = (f32[1600]{0:T(1024)S(1)}, f32[1600]{0:T(1024)}, u32[]{:S(2)}) copy-start(f32[1600]{0:T(1024)} %param.8) | copy-start | bytes 19204
  7.2 64.9 %all-gather.8.cloned.1.call-start = ((), (), s32[]{:S(2)}) async-start(), calls=%async_computation | async-start | bytes 3686400 | tf_op jit(solution)/shard_map/all_gather | solution.py:28
  7.9 154.4 %all-gather.10.cloned.1.call-start = ((), (), s32[]{:S(2)}) async-start(), calls=%async_computation.1 | async-start | bytes 6922240 | tf_op jit(solution)/shard_map/all_gather | solution.py:41
  72.1 90.2 %copy-start = (bf16[1024,1600]{0,1:T(8,128)(2,1)S(1)}, bf16[1024,1600]{0,1:T(8,128)(2,1)}, u32[]{:S(2)}) copy-start(bf16[1024,1600]{0,1:T(8,128)(2,1)} %all-gather.8.cloned.1.call-done) | copy-start | bytes 9830404
  162.3 3.8 %copy-start.2 = (bf16[2048,1600]{1,0:T(8,128)(2,1)S(1)}, bf16[2048,1600]{1,0:T(8,128)(2,1)}, u32[]{:S(2)}) copy-start(bf16[2048,1600]{1,0:T(8,128)(2,1)} %all-gather.10.cloned.1.call-done) | copy-start | bytes 19660804
  172.9 103.7 %copy-start.1 = (s32[128]{0:T(128)S(1)}, s32[128]{0:T(128)}, u32[]{:S(2)}) copy-start(s32[128]{0:T(128)} %param.11) | copy-start | bytes 1540
Sparse Core Ops, SparseCore 0:
  10.0 62.0 all-gather.7
  75.4 86.8 all-gather.9
where the time goes:
time: 284 us
  waiting for transfers between devices  136 us (48%)
  blocking collectives  115 us (40%)
  between operations  14.2 us (5%)
  matrix products  10.6 us (4%)
  other arithmetic  7.67 us (3%)
    all_gather x4, blocking collectives, merged_2(): pieces = jax.tree.map(lambda part: lax.all_gather(part, axis), value)  98.8 us
    all_gather x1, waiting for transfers between devices, on_device(): whole = lax.all_gather(unembed, 'req', axis=0, tiled=True)  87.4 us
    all_gather x1, waiting for transfers between devices, on_device(): lax.all_gather(hidden, 'voc', axis=0, tiled=True)  46.9 us
    all_gather x1, blocking collectives, on_device(): lax.all_gather(targets, 'voc', axis=0, tiled=True)  16.5 us
    dot_general x4, matrix products, on_device(): lax.dot_general(normed, piece, (((1,), (1,)), ((), ())), preferred_elemen...  10.6 us
  transfers between devices with their start and end apart: 2, of which 2 were waited for; matrix products, arithmetic and copies ran while one was open for 1% of the time, Pallas kernels for 0%

commit v1 on v0

--- a/solution.py
+++ b/solution.py
@@ -2,6 +2,7 @@
 import jax.numpy as jnp
 from jax import lax
 from jax.sharding import PartitionSpec as P
+from jax.lax import all_to_all, axis_size
 
 
 def merged_2(value, axis, join):
@@ -25,7 +26,15 @@
 
 def on_device(hidden, norm_gain, unembed, targets, live):
     rows, wanted = (
-        lax.all_gather(hidden, "voc", axis=0, tiled=True),
+        jnp.concatenate(
+            all_to_all(
+                jnp.stack([hidden for _ in range(axis_size("voc"))], 0),
+                "voc",
+                concat_axis=0,
+                split_axis=0,
+            ),
+            0,
+        ),
         lax.all_gather(targets, "voc", axis=0, tiled=True),
     )
     wide = rows.astype(jnp.float32)

time: 284 us -> 227 us (0.80)
  the two profiles are of different devices: /device:TPU:16 before, /device:TPU:192 now
where the time goes in v1:
time: 227 us; the launch traced here: 226 us
  blocking collectives  181 us (80%)
  between operations  14.2 us (6%)
  matrix products  10.9 us (5%)
  other arithmetic  7.98 us (4%)
  starting transfers between devices  7.27 us (3%)
  local copies, waits for them, and re-layouts  4.18 us (2%)
    all_gather x4, blocking collectives, merged_2(): pieces = jax.tree.map(lambda part: lax.all_gather(part, axis), value)  97.8 us
    all_gather x1, blocking collectives, on_device(): lax.all_gather(targets, 'voc', axis=0, tiled=True)  82.9 us
    dot_general x4, matrix products, on_device(): lax.dot_general(normed, piece, (((1,), (1,)), ((), ())), preferred_elemen...  10.9 us
    all_to_all x1, starting transfers between devices, on_device(): all_to_all(jnp.stack([hidden for _ in range(axis_size('voc'))], 0), 'voc'...  7.23 us
  transfers between devices with their start and end apart: 2, of which 0 were waited for; matrix products, arithmetic and copies ran while one was open for 3% of the time, Pallas kernels for 0%

profile of v1, /device:TPU:192, one launch (start us, length us, event | category | flops | bytes accessed | tf_op | source)
XLA Modules:
  0.0 226.3 jit_solution(15937294179767699793)
XLA Ops:
  7.2 0.0 all-gather.7.cloned.1.call-start
  7.2 0.7 all-gather.7.cloned.1.call-update
  7.9 3.2 %stack.2 = bf16[8,128,1600]{1,2,0:T(8,128)(2,1)} broadcast(bf16[128,1600]{0,1:T(8,128)(2,1)} %param.7), dimensions={1,2} | broadcast | bytes 3686400 | tf_op jit(solution)/shard_map/stack | solution.py:31
  11.1 0.0 copy-start.2
  11.1 7.2 %all-to-all-start = ((bf16[8,128,1600]{1,2,0:T(8,128)(2,1)}), bf16[8,128,1600]{1,2,0:T(8,128)(2,1)S(1)}, u32[]{:S(2)}, u32[]{:S(2)}) async-start(bf16[8,128,1600]{1,2,0:T(8,128)(2,1)} %stack.2), calls=%async_computation | async-start | bytes 6553600 | tf_op jit(solution)/shard_map/all_to_all | solution.py:30
  18.3 0.0 copy-start.1
  18.3 0.0 copy-done.2
  18.3 82.9 %all-gather.4 = s32[8,1,128]{2,1,0:T(1,128)S(1)} all-gather(s32[1,1,128]{2,1,0:T(1,128)S(1)} %bitcast.89), channel_id=1, replica_groups=mesh['req'=64,'voc'=8] {'voc'}, dimensions={0}, use_global_device_ids=true | all-gather | bytes 4608 | tf_op jit(solution)/shard_map/all_gather | solution.py:38
  101.2 0.0 all-to-all-done
  101.2 0.6 fusion
  101.9 0.0 copy-done.1
  101.9 2.5 %fusion.2 = bf16[1024,1600]{0,1:T(8,128)(2,1)} fusion(f32[1600]{0:T(1024)S(1)} %copy-done.1, f32[1024]{0:T(1024)S(1)} %rsqrt_bitcast_fusion, bf16[8,128,1600]{1,2,0:T(8,128)(2,1)S(1)} %all-to-all-done), kind=kLoop, calls=%fused_computation.11 | loop fusion | flops 6553600 | bytes 6564096 | tf_op jit(solution)/shard_map/convert_element_type | solution.py:43
  104.4 0.0 copy-start
  104.4 0.0 all-gather.7.cloned.1.call-done
  104.4 0.0 copy-start.4
  104.4 4.7 %fusion.40 = (f32[1024]{0:T(1024)S(1)}, f32[1024,512]{0,1:T(8,128)S(1)}) fusion(bf16[1024,1600]{0,1:T(8,128)(2,1)} %fusion.2, bf16[2048,1600]{1,0:T(8,128)(2,1)} %all-gather.7.cloned.1.call-done), kind=kOutput, calls=%fused_computation.104 | convolution fusion | flops 1678244864 | bytes 7081984 | tf_op jit(solution)/shard_map/dot_general | solution.py:55
  109.0 0.0 copy-done
  109.1 0.7 copy-done.4
  109.8 2.1 fusion.41
  111.9 2.1 fusion.42
  113.9 2.1 fusion.43
  116.0 0.0 copy-start.3
  116.0 3.9 %fusion.3 = (f32[1024]{0:T(1024)S(1)}, f32[1024]{0:T(1024)S(1)}, f32[1024]{0:T(1024)S(1)}, f32[1024]{0:T(1024)S(1)}, f32[1024]{0:T(1024)S(1)}, /*index=5*/f32[10...) fusion(f32[1024,512]{0,1:T(8,128)S(1)} %get-tuple-element.108, ...), kind=kLoop, calls=%fused_computation.20 | loop fusion | flops 14667776 | bytes 8466432 | tf_op jit(solution)/shard_map/reduce_sum | solution.py:64
  120.0 24.5 %all-gather = f32[8192]{0:T(1024)S(1)} all-gather(f32[1024]{0:T(1024)S(1)} %add_add_fusion), channel_id=2, replica_groups=mesh['req'=64,'voc'=8] {'voc'}, dimensions={0}, use_global_device_ids=true | all-gather | bytes 36864 | tf_op jit(solution)/shard_map/all_gather | solution.py:9
  144.4 0.1 add_bitcast_fusion
  144.6 24.5 %all-gather.1 = f32[8,1,1024]{2,1,0:T(1,128)S(1)} all-gather(f32[1,1,1024]{2,1,0:T(1,128)S(1)} %get-tuple-element.95), channel_id=1, replica_groups=mesh['req'=64,'voc'=8] {'voc'}, dimensions={0}, use_global_device_ids=true | all-gather | bytes 36864 | tf_op jit(solution)/shard_map/all_gather | solution.py:9
  169.0 24.5 %all-gather.2 = f32[8,1,1024]{2,1,0:T(1,128)S(1)} all-gather(f32[1,1,1024]{2,1,0:T(1,128)S(1)} %get-tuple-element.94), channel_id=1, replica_groups=mesh['req'=64,'voc'=8] {'voc'}, dimensions={0}, use_global_device_ids=true | all-gather | bytes 36864 | tf_op jit(solution)/shard_map/all_gather | solution.py:9
  193.5 24.5 %all-gather.3 = f32[8,1,1024]{2,1,0:T(1,128)S(1)} all-gather(f32[1,1,1024]{2,1,0:T(1,128)S(1)} %get-tuple-element.88), channel_id=1, replica_groups=mesh['req'=64,'voc'=8] {'voc'}, dimensions={0}, use_global_device_ids=true | all-gather | bytes 36864 | tf_op jit(solution)/shard_map/all_gather | solution.py:9
  218.0 0.8 while.16
  218.8 0.0 copy-done.3
  218.8 0.6 subtract_multiply_fusion
  (59 shorter events, 0.5 us)
Async XLA Ops:
  7.2 97.2 %all-gather.7.cloned.1.call-start = ((), (), s32[]{:S(2)}) async-start(), calls=%async_computation.1 | async-start | bytes 6922240 | tf_op jit(solution)/shard_map/all_gather | solution.py:50
  11.1 7.2 %copy-start.2 = (s32[128]{0:T(128)S(1)}, s32[128]{0:T(128)}, u32[]{:S(2)}) copy-start(s32[128]{0:T(128)} %param.10) | copy-start | bytes 1540
  11.1 90.1 %all-to-all-start = ((bf16[8,128,1600]{1,2,0:T(8,128)(2,1)}), bf16[8,128,1600]{1,2,0:T(8,128)(2,1)S(1)}, u32[]{:S(2)}, u32[]{:S(2)}) async-start(bf16[8,128,1600]{1,2,0:T(8,128)(2,1)} %stack.2), calls=%async_computation | async-start | bytes 6553600 | tf_op jit(solution)/shard_map/all_to_all | solution.py:30
  18.3 83.6 %copy-start.1 = (f32[1600]{0:T(1024)S(1)}, f32[1600]{0:T(1024)}, u32[]{:S(2)}) copy-start(f32[1600]{0:T(1024)} %param.8) | copy-start | bytes 19204
  104.4 4.7 %copy-start = (bf16[1024,1600]{0,1:T(8,128)(2,1)S(1)}, bf16[1024,1600]{0,1:T(8,128)(2,1)}, u32[]{:S(2)}) copy-start(bf16[1024,1600]{0,1:T(8,128)(2,1)} %fusion.2) | copy-start | bytes 9830404
  104.4 5.4 %copy-start.4 = (bf16[2048,1600]{1,0:T(8,128)(2,1)S(1)}, bf16[2048,1600]{1,0:T(8,128)(2,1)}, u32[]{:S(2)}) copy-start(bf16[2048,1600]{1,0:T(8,128)(2,1)} %all-gather.7.cloned.1.call-done) | copy-start | bytes 19660804
  116.0 102.8 %copy-start.3 = (s32[128]{0:T(128)S(1)}, s32[128]{0:T(128)}, u32[]{:S(2)}) copy-start(s32[128]{0:T(128)} %param.11) | copy-start | bytes 1540
Sparse Core Ops, SparseCore 0:
  11.3 88.6 all-gather.6
